TPU v7x, 32 devices: a whole 2x2x4 slice. The times are simulated.
32 devices in a mesh: groups: 2 (over x), seq: 16 (over z, y, core).
Axes of the slice: x: 2, y: 2, z: 4, core: 2. Of those that a mesh axis runs over, the one named last changes fastest.
Arguments:
- video_q: bfloat16 [16384, 2048], P(('groups', 'seq')), parts along dimension 0, may hold values from -64 to 64
- video_k: bfloat16 [16384, 2048], P(('groups', 'seq')), parts along dimension 0, may hold values from -6 to 6
- video_v: bfloat16 [16384, 2048], P(('groups', 'seq')), parts along dimension 0, may hold values from -4 to 4
- audio_q: bfloat16 [256, 2048], P(('groups', 'seq')), parts along dimension 0, may hold values from -64 to 64
- audio_k: bfloat16 [256, 2048], P(('groups', 'seq')), parts along dimension 0, may hold values from -6 to 6
- audio_v: bfloat16 [256, 2048], P(('groups', 'seq')), parts along dimension 0, may hold values from -4 to 4
Outputs:
- video_out: bfloat16 [16384, 2048], P(('groups', 'seq')), parts along dimension 0
- audio_out: bfloat16 [256, 2048], P(('groups', 'seq')), parts along dimension 0
There are 2 independent parts, one for each index of `groups`. A program takes and returns all parts, laid end to end along the dimension named above; each array names one. Nothing has to cross between parts.
All inputs are finite; a program needn't handle non-finite values.
Results may differ from a plain program's by a relative error of at most 0.007.
Values may be sent and summed in bfloat16 or wider, within the bound.
No kernel may reach another device: no remote copies, remote signals or barrier semaphores. Data moves between devices by JAX's collectives and lax.ppermute only.
A program may use at most 128 MiB of HBM per device.

v0:
```python
import math
import jax
import jax.numpy as jnp
from jax import lax
from jax.sharding import PartitionSpec as P

lowest_score = -1e30


def spread(scales):
    return jnp.repeat(scales, 64, axis=1)


def partial_block(queries, keys, values):
    head_count = queries.shape[1] // 64
    query_heads = queries.reshape(queries.shape[0], head_count, 64)
    key_heads = keys.reshape(keys.shape[0], head_count, 64)
    value_heads = values.reshape(values.shape[0], head_count, 64)
    scores = (
        jnp.einsum("rhd,shd->hrs", query_heads, key_heads, preferred_element_type=jnp.float32)
        * 0.125
    )
    highest = jnp.max(scores, axis=2)
    weights = jnp.exp(scores - highest[:, :, None])
    totals = jnp.sum(weights, axis=2)
    summed = jnp.einsum(
        "hrs,shd->rhd",
        weights.astype(jnp.bfloat16),
        value_heads,
        preferred_element_type=jnp.float32,
    )
    return (highest.T, totals.T, summed.reshape(queries.shape[0], head_count * 64))


def combine(earlier, later):
    highest = jnp.maximum(earlier[0], later[0])
    earlier_scale = jnp.exp(earlier[0] - highest)
    later_scale = jnp.exp(later[0] - highest)
    totals = earlier[1] * earlier_scale + later[1] * later_scale
    summed = earlier[2] * spread(earlier_scale) + later[2] * spread(later_scale)
    return (highest, totals, summed)


def blocked_partial(queries, keys, values):
    row_count = queries.shape[0]
    model_width = queries.shape[1]
    block_rows = math.gcd(row_count, 128)
    stacked = queries.reshape(row_count // block_rows, block_rows, model_width)
    newest = lax.map(lambda query_rows: partial_block(query_rows, keys, values), stacked)
    return tuple((member.reshape(row_count, member.shape[2]) for member in newest))


def empty_state(row_count, model_width):
    head_count = model_width // 64
    return (
        jnp.full((row_count, head_count), lowest_score, jnp.float32),
        jnp.zeros((row_count, head_count), jnp.float32),
        jnp.zeros((row_count, model_width), jnp.float32),
    )


def local(video_q, video_k, video_v, audio_q, audio_k, audio_v):
    tok_rows = video_q.shape[0]
    model_width = video_q.shape[1]
    pieces = (
        lax.all_gather(audio_k, "seq", axis=0, tiled=True),
        lax.all_gather(audio_v, "seq", axis=0, tiled=True),
    )
    newest = blocked_partial(video_q, pieces[0], pieces[1])
    highest, totals, summed = combine(empty_state(tok_rows, model_width), newest)
    video_out = (summed / spread(totals)).astype(jnp.bfloat16)
    key_heads, value_heads, query_heads = (
        lax.all_to_all(video_k, "seq", split_axis=1, concat_axis=0, tiled=True),
        lax.all_to_all(video_v, "seq", split_axis=1, concat_axis=0, tiled=True),
        lax.all_to_all(audio_q, "seq", split_axis=1, concat_axis=0, tiled=True),
    )
    total_keys = key_heads.shape[0]
    columns = key_heads.shape[1]
    key_block = math.gcd(total_keys, 4096)
    block_count = total_keys // key_block

    def advance(running, pieces):
        return (combine(running, partial_block(query_heads, pieces[0], pieces[1])), None)

    state, ignored = lax.scan(
        advance,
        empty_state(query_heads.shape[0], columns),
        (
            key_heads.reshape(block_count, key_block, columns),
            value_heads.reshape(block_count, key_block, columns),
        ),
    )
    head_out = (state[2] / spread(state[1])).astype(jnp.bfloat16)
    audio_out = lax.all_to_all(head_out, "seq", split_axis=0, concat_axis=1, tiled=True)
    return (video_out, audio_out)


def solution(mesh):
    placed = (
        P(("groups", "seq"), None),
        P(("groups", "seq"), None),
        P(("groups", "seq"), None),
        P(("groups", "seq"), None),
        P(("groups", "seq"), None),
        P(("groups", "seq"), None),
    )
    return jax.shard_map(
        local,
        mesh=mesh,
        in_specs=placed,
        out_specs=(P(("groups", "seq"), None), P(("groups", "seq"), None)),
        check_vma=False,
    )
```

profile of v0, /device:TPU:0, one launch (start us, length us, event | category | flops | bytes accessed | tf_op | source)
XLA Modules:
  0.0 264.3 jit_solution(13597468701080333482)
XLA Ops:
  0.6 7.4 %all-to-all-start.1 = ((bf16[8,16,128]{2,0,1:T(8,128)(2,1)}), bf16[8,16,128]{2,0,1:T(8,128)(2,1)S(1)}, u32[]{:S(2)}, u32[]{:S(2)}) async-start(bf16[8,16,128]{2,0,1:T(8,128)(2,1)} %bitcast.158), calls=%async_computation.1 | async-start | bytes 65536 | tf_op jit(solution)/shard_map/all_to_all | solution.py:75
  8.0 3.9 %copy.57 = bf16[512,2048]{0,1:T(8,128)(2,1)} copy(bf16[512,2048]{1,0:T(8,128)(2,1)} %param.11) | data formatting | bytes 4194304 | tf_op args[1]
  12.0 2.7 %all-to-all-done.1 = bf16[8,16,128]{2,0,1:T(8,128)(2,1)S(1)} async-done(((bf16[8,16,128]{2,0,1:T(8,128)(2,1)}), bf16[8,16,128]{2,0,1:T(8,128)(2,1)S(1)}, u32[]{:S(2)}, u32[]{:S(2)}) %all-to-all-start.1) | async-done | bytes 32800 | tf_op jit(solution)/shard_map/all_to_all | solution.py:75
  14.7 4.6 %all-to-all-start = ((bf16[512,16,128]{0,2,1:T(8,128)(2,1)}), bf16[512,16,128]{0,2,1:T(8,128)(2,1)}, u32[]{:S(2)}, u32[]{:S(2)}) async-start(bf16[512,16,128]{0,2,1:T(8,128)(2,1)} %bitcast.13), calls=%async_computation | async-start | bytes 4194304 | tf_op jit(solution)/shard_map/all_to_all | solution.py:73
  19.3 56.4 %all_gather.6 = bf16[128,2048]{1,0:T(8,128)(2,1)S(1)} all-gather(bf16[8,2048]{1,0:T(8,128)(2,1)S(1)} %copy-done.1), channel_id=1, replica_groups=mesh['groups'=2,'seq'=16] {'seq'}, dimensions={0}, use_global_device_ids=true | all-gather | bytes 557056 | tf_op jit(solution)/shard_map/all_gather | solution.py:66
  76.0 25.5 %all_gather.7 = bf16[128,2048]{1,0:T(8,128)(2,1)} all-gather(bf16[8,2048]{1,0:T(8,128)(2,1)S(1)} %copy-done.2), channel_id=1, replica_groups=mesh['groups'=2,'seq'=16] {'seq'}, dimensions={0}, use_global_device_ids=true | all-gather | bytes 557056 | tf_op jit(solution)/shard_map/all_gather | solution.py:67
  101.5 1.3 copy.53
  102.9 2.6 copy.59
  105.4 4.5 %all-to-all-start.2 = ((bf16[512,16,128]{0,2,1:T(8,128)(2,1)}), bf16[512,16,128]{0,2,1:T(8,128)(2,1)}, u32[]{:S(2)}, u32[]{:S(2)}) async-start(bf16[512,16,128]{0,2,1:T(8,128)(2,1)} %bitcast.19), calls=%async_computation.2 | async-start | bytes 4194304 | tf_op jit(solution)/shard_map/all_to_all | solution.py:74
  109.9 122.1 %while.29 = (s32[]{:T(128)}, f32[4,128,32]{1,0,2:T(4,128)S(1)}, f32[4,128,32]{1,0,2:T(4,128)S(1)}, f32[4,128,2048]{1,0,2:T(4,128)}, bf16[4,128,2048]{2,1,0:T(8,1...) while((s32[]{:T(128)}, f32[4,128,32]{1,0,2:T(4,128)S(1)}, ...), condition=%wide.region_3.4_spmd, body=%wide.region_0.3_spmd.sunk | while | flops 138403840 | bytes 13238389 | solution.py:49
  109.9 1.1 constant_dynamic-slice_fusion.5
  112.9 27.5 %dynamic_update_slice.16 = f32[4,128,2048]{1,0,2:T(4,128)} dynamic-update-slice(f32[4,128,2048]{1,0,2:T(4,128)} %get-tuple-element.322, f32[1,128,2048]{1,0,2:T(1,128)S(1)} %bitcast.142, s32[]{:T(128)S(6)} %copy.101, s32[]{:T(128)} %constant.28.clone.1..sunk, s32[]{:T(128)} %constant.28.clone.1..sunk) | dynamic-update-slice | bytes 2097156 | tf_op jit(solution)/shard_map/while/body/jit(dynamic_update_index_in_dim)/dynamic_update_slice | solution.py:49
  143.4 27.5 %dynamic_update_slice.16 = f32[4,128,2048]{1,0,2:T(4,128)} dynamic-update-slice(f32[4,128,2048]{1,0,2:T(4,128)} %get-tuple-element.322, f32[1,128,2048]{1,0,2:T(1,128)S(1)} %bitcast.142, s32[]{:T(128)S(6)} %copy.101, s32[]{:T(128)} %constant.28.clone.1..sunk, s32[]{:T(128)} %constant.28.clone.1..sunk) | dynamic-update-slice | bytes 2097156 | tf_op jit(solution)/shard_map/while/body/jit(dynamic_update_index_in_dim)/dynamic_update_slice | solution.py:49
  173.9 27.5 %dynamic_update_slice.16 = f32[4,128,2048]{1,0,2:T(4,128)} dynamic-update-slice(f32[4,128,2048]{1,0,2:T(4,128)} %get-tuple-element.322, f32[1,128,2048]{1,0,2:T(1,128)S(1)} %bitcast.142, s32[]{:T(128)S(6)} %copy.101, s32[]{:T(128)} %constant.28.clone.1..sunk, s32[]{:T(128)} %constant.28.clone.1..sunk) | dynamic-update-slice | bytes 2097156 | tf_op jit(solution)/shard_map/while/body/jit(dynamic_update_index_in_dim)/dynamic_update_slice | solution.py:49
  204.4 27.5 %dynamic_update_slice.16 = f32[4,128,2048]{1,0,2:T(4,128)} dynamic-update-slice(f32[4,128,2048]{1,0,2:T(4,128)} %get-tuple-element.322, f32[1,128,2048]{1,0,2:T(1,128)S(1)} %bitcast.142, s32[]{:T(128)S(6)} %copy.101, s32[]{:T(128)} %constant.28.clone.1..sunk, s32[]{:T(128)} %constant.28.clone.1..sunk) | dynamic-update-slice | bytes 2097156 | tf_op jit(solution)/shard_map/while/body/jit(dynamic_update_index_in_dim)/dynamic_update_slice | solution.py:49
  232.1 3.9 %copy.58 = bf16[16,512,128]{2,1,0:T(8,128)(2,1)} copy(bf16[16,512,128]{1,2,0:T(8,128)(2,1)} %bitcast.14) | data formatting | bytes 4194304 | tf_op jit(solution)/shard_map/all_to_all | solution.py:73
  236.0 3.9 %copy.60 = bf16[16,512,128]{2,1,0:T(8,128)(2,1)} copy(bf16[16,512,128]{1,2,0:T(8,128)(2,1)} %bitcast.20) | data formatting | bytes 4194304 | tf_op jit(solution)/shard_map/all_to_all | solution.py:74
  239.9 10.5 %while.30 = (s32[]{:T(128)}, f32[128,2]{0,1:T(2,128)S(1)}, f32[128,2]{0,1:T(2,128)S(1)}, f32[128,128]{0,1:T(8,128)S(1)}, bf16[2,4096,128]{2,1,0:T(8,128)(2,1)}, ...) while((s32[]{:T(128)}, f32[128,2]{0,1:T(2,128)S(1)}, ...), condition=%wide.region_7.8_spmd.clone, body=%wide.region_4.7_spmd.clone.sunk | while | flops 274793984 | bytes 23378036 | solution.py:85
  239.9 1.7 constant_dynamic-slice_fusion.6
  245.2 1.7 constant_dynamic-slice_fusion.6
  251.2 5.9 %all-to-all-start.3 = ((bf16[16,8,128]{2,1,0:T(8,128)(2,1)}), bf16[16,8,128]{2,1,0:T(8,128)(2,1)S(1)}, u32[]{:S(2)}, u32[]{:S(2)}) async-start(bf16[16,8,128]{2,1,0:T(8,128)(2,1)} %bitcast.23), calls=%async_computation.3 | async-start | bytes 65536 | tf_op jit(solution)/shard_map/all_to_all | solution.py:94
  257.1 2.9 %fusion.23 = bf16[512,2048]{0,1:T(8,128)(2,1)S(1)} fusion(f32[256,8,4,128]{3,2,1,0:T(4,128)} %bitcast.150, f32[512,32]{0,1:T(8,128)S(1)} %get-tuple-element.202, f32[512,32]{0,1:T(8,128)S(1)} %get-tuple-element.203, f32[512,32]{0,1:T(8,128)S(1)} %get-tuple-element.201), kind=kLoop, calls=%fused_computation.33 | loop fusion | flops 4194304 | bytes 6488064 | tf_op jit(solution)/shard_map/convert_element_type | solution.py:71
  260.0 2.4 copy.65
  262.4 1.3 all-to-all-done.3
  (61 shorter events, 19.6 us)
Async XLA Ops:
  0.6 14.0 %all-to-all-start.1 = ((bf16[8,16,128]{2,0,1:T(8,128)(2,1)}), bf16[8,16,128]{2,0,1:T(8,128)(2,1)S(1)}, u32[]{:S(2)}, u32[]{:S(2)}) async-start(bf16[8,16,128]{2,0,1:T(8,128)(2,1)} %bitcast.158), calls=%async_computation.1 | async-start | bytes 65536 | tf_op jit(solution)/shard_map/all_to_all | solution.py:75
  14.7 4.6 %copy-start.1 = (bf16[8,2048]{1,0:T(8,128)(2,1)S(1)}, bf16[8,2048]{1,0:T(8,128)(2,1)}, u32[]{:S(2)}) copy-start(bf16[8,2048]{1,0:T(8,128)(2,1)} %param.14) | copy-start | bytes 98308
  14.7 61.4 %copy-start.2 = (bf16[8,2048]{1,0:T(8,128)(2,1)S(1)}, bf16[8,2048]{1,0:T(8,128)(2,1)}, u32[]{:S(2)}) copy-start(bf16[8,2048]{1,0:T(8,128)(2,1)} %param.15) | copy-start | bytes 98308
  14.7 90.8 %all-to-all-start = ((bf16[512,16,128]{0,2,1:T(8,128)(2,1)}), bf16[512,16,128]{0,2,1:T(8,128)(2,1)}, u32[]{:S(2)}, u32[]{:S(2)}) async-start(bf16[512,16,128]{0,2,1:T(8,128)(2,1)} %bitcast.13), calls=%async_computation | async-start | bytes 4194304 | tf_op jit(solution)/shard_map/all_to_all | solution.py:73
  19.2 83.6 %copy-start = (bf16[512,2048]{1,0:T(8,128)(2,1)S(1)}, bf16[512,2048]{1,0:T(8,128)(2,1)}, u32[]{:S(2)}) copy-start(bf16[512,2048]{1,0:T(8,128)(2,1)} %param.12) | copy-start | bytes 6291460
  105.4 130.6 %all-to-all-start.2 = ((bf16[512,16,128]{0,2,1:T(8,128)(2,1)}), bf16[512,16,128]{0,2,1:T(8,128)(2,1)}, u32[]{:S(2)}, u32[]{:S(2)}) async-start(bf16[512,16,128]{0,2,1:T(8,128)(2,1)} %bitcast.19), calls=%async_computation.2 | async-start | bytes 4194304 | tf_op jit(solution)/shard_map/all_to_all | solution.py:74
  251.2 12.5 %all-to-all-start.3 = ((bf16[16,8,128]{2,1,0:T(8,128)(2,1)}), bf16[16,8,128]{2,1,0:T(8,128)(2,1)S(1)}, u32[]{:S(2)}, u32[]{:S(2)}) async-start(bf16[16,8,128]{2,1,0:T(8,128)(2,1)} %bitcast.23), calls=%async_computation.3 | async-start | bytes 65536 | tf_op jit(solution)/shard_map/all_to_all | solution.py:94
where the time goes:
time: 268 us; the launch traced here: 264 us
  local copies, waits for them, and re-layouts  142 us (53%)
  blocking collectives  81.9 us (31%)
  starting transfers between devices  22.3 us (8%)
  matrix products  7.69 us (3%)
  other arithmetic  5.8 us (2%)
  waiting for transfers between devices  4.06 us (2%)
    dynamic_update_slice x12, local copies, waits for them, and re-layouts, blocked_partial(): lax.map(lambda query_rows: partial_block(query_rows, keys, values), stacked)  111 us
    all_gather x1, blocking collectives, local(): lax.all_gather(audio_k, 'seq', axis=0, tiled=True)  56.4 us
    all_gather x1, blocking collectives, local(): lax.all_gather(audio_v, 'seq', axis=0, tiled=True)  25.5 us
    unnamed x11, local copies, waits for them, and re-layouts  9.6 us
    all_to_all x1, starting transfers between devices, local(): lax.all_to_all(audio_q, 'seq', split_axis=1, concat_axis=0, tiled=True)  7.4 us
    all_to_all x1, starting transfers between devices, local(): lax.all_to_all(head_out, 'seq', split_axis=0, concat_axis=1, tiled=True)  5.89 us
    dynamic_slice x6, local copies, waits for them, and re-layouts, local(): lax.scan(advance, empty_state(query_heads.shape[0], columns), (key_heads....  5.49 us
    dynamic_slice x8, local copies, waits for them, and re-layouts, blocked_partial(): lax.map(lambda query_rows: partial_block(query_rows, keys, values), stacked)  5.4 us
  transfers between devices with their start and end apart: 4, of which 2 were waited for; matrix products, arithmetic and copies ran while one was open for 53% of the time, Pallas kernels for 0%

commit v1 on v0

--- a/solution.py
+++ b/solution.py
@@ -69,9 +69,18 @@
     newest = blocked_partial(video_q, pieces[0], pieces[1])
     highest, totals, summed = combine(empty_state(tok_rows, model_width), newest)
     video_out = (summed / spread(totals)).astype(jnp.bfloat16)
+    row_write = lambda x_local, link_axis, dim_at, d_out: jnp.concatenate(
+        lax.all_to_all(
+            jnp.stack(jnp.split(x_local, lax.axis_size(link_axis), axis=dim_at)),
+            axis_name=link_axis,
+            split_axis=0,
+            concat_axis=0,
+        ),
+        axis=d_out,
+    )
     key_heads, value_heads, query_heads = (
         lax.all_to_all(video_k, "seq", split_axis=1, concat_axis=0, tiled=True),
-        lax.all_to_all(video_v, "seq", split_axis=1, concat_axis=0, tiled=True),
+        row_write(video_v, "seq", 1, 0),
         lax.all_to_all(audio_q, "seq", split_axis=1, concat_axis=0, tiled=True),
     )
     total_keys = key_heads.shape[0]

time: 268 us -> 298 us (1.11)
  local copies, waits for them, and re-layouts: 142 us -> 166 us
  matrix products: 7.69 us -> 16 us
    all_gather x1, blocking collectives: 56.4 us -> 23.5 us  [local(): lax.all_gather(audio_k, 'seq', axis=0, tiled=True)]
    all_gather x1, blocking collectives: 25.5 us -> 56.6 us  [local(): lax.all_gather(audio_v, 'seq', axis=0, tiled=True)]
    unnamed x11 -> x23, local copies, waits for them, and re-layouts: 9.6 us -> 31.7 us
    dot_general x6, matrix products: 3.77 us -> 7.94 us  [partial_block(): jnp.einsum('hrs,shd->rhd', weights.astype(jnp.bfloat16), value_heads, pre...]
    dot_general x6, matrix products: 3.92 us -> 8.09 us  [partial_block(): jnp.einsum('rhd,shd->hrs', query_heads, key_heads, preferred_element_type...]
    all_to_all x1 -> x0, local copies, waits for them, and re-layouts: 3.91 us -> none  [local(): lax.all_to_all(video_v, 'seq', split_axis=1, concat_axis=0, tiled=True)]
    while x0 -> x8, local copies, waits for them, and re-layouts: none -> 3.89 us
  transfers between devices with their start and end apart: 4 -> 4, of which waited for: 2 -> 1; matrix products, arithmetic and copies ran while one was open for 53% -> 58% of each run, Pallas kernels for 0% -> 0%
where the time goes in v1:
time: 298 us; the launch traced here: 294 us
  local copies, waits for them, and re-layouts  166 us (56%)
  blocking collectives  80 us (27%)
  starting transfers between devices  24.2 us (8%)
  matrix products  16 us (5%)
  other arithmetic  5.8 us (2%)
    dynamic_update_slice x12, local copies, waits for them, and re-layouts, blocked_partial(): lax.map(lambda query_rows: partial_block(query_rows, keys, values), stacked)  111 us
    all_gather x1, blocking collectives, local(): lax.all_gather(audio_v, 'seq', axis=0, tiled=True)  56.6 us
    unnamed x23, local copies, waits for them, and re-layouts  31.7 us
    all_gather x1, blocking collectives, local(): lax.all_gather(audio_k, 'seq', axis=0, tiled=True)  23.5 us
    dot_general x6, matrix products, partial_block(): jnp.einsum('rhd,shd->hrs', query_heads, key_heads, preferred_element_type...  8.09 us
    dot_general x6, matrix products, partial_block(): jnp.einsum('hrs,shd->rhd', weights.astype(jnp.bfloat16), value_heads, pre...  7.94 us
    all_to_all x1, starting transfers between devices, local(): lax.all_to_all(audio_q, 'seq', split_axis=1, concat_axis=0, tiled=True)  7.4 us
    all_to_all x1, starting transfers between devices, local(): lax.all_to_all(jnp.stack(jnp.split(x_local, lax.axis_size(link_axis), axi...  6.94 us
  transfers between devices with their start and end apart: 4, of which 1 were waited for; matrix products, arithmetic and copies ran while one was open for 58% of the time, Pallas kernels for 0%

profile of v1, /device:TPU:0, one launch (start us, length us, event | category | flops | bytes accessed | tf_op | source)
XLA Modules:
  0.0 293.9 jit_solution(12636935950401744175)
XLA Ops:
  0.6 7.4 %all-to-all-start.1 = ((bf16[8,16,128]{2,0,1:T(8,128)(2,1)}), bf16[8,16,128]{2,0,1:T(8,128)(2,1)S(1)}, u32[]{:S(2)}, u32[]{:S(2)}) async-start(bf16[8,16,128]{2,0,1:T(8,128)(2,1)} %bitcast.188), calls=%async_computation.1 | async-start | bytes 65536 | tf_op jit(solution)/shard_map/all_to_all | solution.py:84
  8.0 23.5 %all_gather.6 = bf16[128,2048]{1,0:T(8,128)(2,1)S(1)} all-gather(bf16[8,2048]{1,0:T(8,128)(2,1)} %param.14), channel_id=1, replica_groups=mesh['groups'=2,'seq'=16] {'seq'}, dimensions={0}, use_global_device_ids=true | all-gather | bytes 557056 | tf_op jit(solution)/shard_map/all_gather | solution.py:66
  32.5 3.9 %copy.55 = bf16[512,2048]{0,1:T(8,128)(2,1)} copy(bf16[512,2048]{1,0:T(8,128)(2,1)} %param.11) | data formatting | bytes 4194304 | tf_op args[1]
  36.4 3.9 %all-to-all-start = ((bf16[512,16,128]{0,2,1:T(8,128)(2,1)}), bf16[512,16,128]{0,2,1:T(8,128)(2,1)S(1)}, u32[]{:S(2)}, u32[]{:S(2)}) async-start(bf16[512,16,128]{0,2,1:T(8,128)(2,1)} %bitcast.178), calls=%async_computation | async-start | bytes 4194304 | tf_op jit(solution)/shard_map/all_to_all | solution.py:82
  40.3 56.6 %all_gather.7 = bf16[128,2048]{1,0:T(8,128)(2,1)S(1)} all-gather(bf16[8,2048]{1,0:T(8,128)(2,1)S(1)} %copy-done.3), channel_id=1, replica_groups=mesh['groups'=2,'seq'=16] {'seq'}, dimensions={0}, use_global_device_ids=true | all-gather | bytes 557056 | tf_op jit(solution)/shard_map/all_gather | solution.py:67
  97.9 1.6 bitcast_dynamic-update-slice_fusion.15
  101.0 1.6 bitcast_dynamic-update-slice_fusion.13
  104.1 1.6 bitcast_dynamic-update-slice_fusion.11
  107.2 1.6 bitcast_dynamic-update-slice_fusion.9
  119.7 1.6 bitcast_dynamic-update-slice_fusion.1
  121.3 1.6 bitcast_dynamic-update-slice_fusion
  124.1 6.9 %all-to-all-start.2 = ((bf16[16,512,128]{2,1,0:T(8,128)(2,1)}), bf16[16,512,128]{2,1,0:T(8,128)(2,1)S(1)}, u32[]{:S(2)}, u32[]{:S(2)}) async-start(bf16[16,512,128]{2,1,0:T(8,128)(2,1)} %bitcast_dynamic-update-slice_fusion), calls=%async_computation.2 | async-start | bytes 4194304 | tf_op jit(solution)/shard_map/all_to_all | solution.py:73
  131.1 130.4 %while.29 = (s32[]{:T(128)}, f32[4,128,32]{1,0,2:T(4,128)S(1)}, f32[4,128,32]{1,0,2:T(4,128)S(1)}, f32[4,128,2048]{1,0,2:T(4,128)}, bf16[4,128,2048]{2,1,0:T(8,1...) while((s32[]{:T(128)}, f32[4,128,32]{1,0,2:T(4,128)S(1)}, ...), condition=%wide.region_3.4_spmd, body=%wide.region_0.3_spmd.sunk | while | flops 138403840 | bytes 13238389 | solution.py:49
  136.2 27.5 %dynamic_update_slice.16 = f32[4,128,2048]{1,0,2:T(4,128)} dynamic-update-slice(f32[4,128,2048]{1,0,2:T(4,128)} %get-tuple-element.322, f32[1,128,2048]{1,0,2:T(1,128)S(1)} %bitcast.172, s32[]{:T(128)S(6)} %copy.97, s32[]{:T(128)} %constant.28.clone.1..sunk, s32[]{:T(128)} %constant.28.clone.1..sunk) | dynamic-update-slice | bytes 2097156 | tf_op jit(solution)/shard_map/while/body/jit(dynamic_update_index_in_dim)/dynamic_update_slice | solution.py:49
  168.7 27.5 %dynamic_update_slice.16 = f32[4,128,2048]{1,0,2:T(4,128)} dynamic-update-slice(f32[4,128,2048]{1,0,2:T(4,128)} %get-tuple-element.322, f32[1,128,2048]{1,0,2:T(1,128)S(1)} %bitcast.172, s32[]{:T(128)S(6)} %copy.97, s32[]{:T(128)} %constant.28.clone.1..sunk, s32[]{:T(128)} %constant.28.clone.1..sunk) | dynamic-update-slice | bytes 2097156 | tf_op jit(solution)/shard_map/while/body/jit(dynamic_update_index_in_dim)/dynamic_update_slice | solution.py:49
  201.3 27.5 %dynamic_update_slice.16 = f32[4,128,2048]{1,0,2:T(4,128)} dynamic-update-slice(f32[4,128,2048]{1,0,2:T(4,128)} %get-tuple-element.322, f32[1,128,2048]{1,0,2:T(1,128)S(1)} %bitcast.172, s32[]{:T(128)S(6)} %copy.97, s32[]{:T(128)} %constant.28.clone.1..sunk, s32[]{:T(128)} %constant.28.clone.1..sunk) | dynamic-update-slice | bytes 2097156 | tf_op jit(solution)/shard_map/while/body/jit(dynamic_update_index_in_dim)/dynamic_update_slice | solution.py:49
  233.9 27.5 %dynamic_update_slice.16 = f32[4,128,2048]{1,0,2:T(4,128)} dynamic-update-slice(f32[4,128,2048]{1,0,2:T(4,128)} %get-tuple-element.322, f32[1,128,2048]{1,0,2:T(1,128)S(1)} %bitcast.172, s32[]{:T(128)S(6)} %copy.97, s32[]{:T(128)} %constant.28.clone.1..sunk, s32[]{:T(128)} %constant.28.clone.1..sunk) | dynamic-update-slice | bytes 2097156 | tf_op jit(solution)/shard_map/while/body/jit(dynamic_update_index_in_dim)/dynamic_update_slice | solution.py:49
  261.6 3.9 %copy.56 = bf16[16,512,128]{2,1,0:T(8,128)(2,1)} copy(bf16[16,512,128]{1,2,0:T(8,128)(2,1)} %bitcast.177) | data formatting | bytes 4194304 | tf_op jit(solution)/shard_map/all_to_all | solution.py:82
  265.5 14.4 %while.30 = (s32[]{:T(128)}, f32[128,2]{0,1:T(2,128)S(1)}, f32[128,2]{0,1:T(2,128)S(1)}, f32[128,128]{0,1:T(8,128)S(1)}, bf16[2,4096,128]{2,1,0:T(8,128)(2,1)}, ...) while((s32[]{:T(128)}, f32[128,2]{0,1:T(2,128)S(1)}, ...), condition=%wide.region_7.8_spmd.clone, body=%wide.region_4.7_spmd.clone.sunk | while | flops 274793984 | bytes 40155304 | solution.py:94
  266.8 1.7 constant_dynamic-slice_fusion.6
  274.0 1.7 constant_dynamic-slice_fusion.6
  280.6 6.0 %all-to-all-start.3 = ((bf16[16,8,128]{2,1,0:T(8,128)(2,1)}), bf16[16,8,128]{2,1,0:T(8,128)(2,1)S(1)}, u32[]{:S(2)}, u32[]{:S(2)}) async-start(bf16[16,8,128]{2,1,0:T(8,128)(2,1)} %bitcast.37), calls=%async_computation.3 | async-start | bytes 65536 | tf_op jit(solution)/shard_map/all_to_all | solution.py:103
  286.7 2.9 fusion.23
  289.5 2.4 copy.61
  (81 shorter events, 52.8 us)
Async XLA Ops:
  0.6 35.8 %all-to-all-start.1 = ((bf16[8,16,128]{2,0,1:T(8,128)(2,1)}), bf16[8,16,128]{2,0,1:T(8,128)(2,1)S(1)}, u32[]{:S(2)}, u32[]{:S(2)}) async-start(bf16[8,16,128]{2,0,1:T(8,128)(2,1)} %bitcast.188), calls=%async_computation.1 | async-start | bytes 65536 | tf_op jit(solution)/shard_map/all_to_all | solution.py:84
  36.4 3.9 %copy-start.3 = (bf16[8,2048]{1,0:T(8,128)(2,1)S(1)}, bf16[8,2048]{1,0:T(8,128)(2,1)}, u32[]{:S(2)}) copy-start(bf16[8,2048]{1,0:T(8,128)(2,1)} %param.15) | copy-start | bytes 98308
  36.4 86.4 %all-to-all-start = ((bf16[512,16,128]{0,2,1:T(8,128)(2,1)}), bf16[512,16,128]{0,2,1:T(8,128)(2,1)S(1)}, u32[]{:S(2)}, u32[]{:S(2)}) async-start(bf16[512,16,128]{0,2,1:T(8,128)(2,1)} %bitcast.178), calls=%async_computation | async-start | bytes 4194304 | tf_op jit(solution)/shard_map/all_to_all | solution.py:82
  122.8 1.3 copy-start.2
  124.1 141.3 %all-to-all-start.2 = ((bf16[16,512,128]{2,1,0:T(8,128)(2,1)}), bf16[16,512,128]{2,1,0:T(8,128)(2,1)S(1)}, u32[]{:S(2)}, u32[]{:S(2)}) async-start(bf16[16,512,128]{2,1,0:T(8,128)(2,1)} %bitcast_dynamic-update-slice_fusion), calls=%async_computation.2 | async-start | bytes 4194304 | tf_op jit(solution)/shard_map/all_to_all | solution.py:73
  265.5 1.3 copy-start
  271.1 1.6 copy-start.1
  272.7 1.3 copy-start
  278.3 1.6 copy-start.1
  280.6 12.6 %all-to-all-start.3 = ((bf16[16,8,128]{2,1,0:T(8,128)(2,1)}), bf16[16,8,128]{2,1,0:T(8,128)(2,1)S(1)}, u32[]{:S(2)}, u32[]{:S(2)}) async-start(bf16[16,8,128]{2,1,0:T(8,128)(2,1)} %bitcast.37), calls=%async_computation.3 | async-start | bytes 65536 | tf_op jit(solution)/shard_map/all_to_all | solution.py:103
